TPU v7x, 128 devices: a whole 4x4x4 slice. The times are simulated.
128 devices in a mesh: dp: 4 (over x), expert: 32 (over y, z, core).
Axes of the slice: x: 4, y: 4, z: 4, core: 2. Of those that a mesh axis runs over, the one named last changes fastest.
Arguments:
- tokens: bfloat16 [16384, 4096], P(('dp', 'expert')), may hold values from -6 to 6
- cotangent: bfloat16 [16384, 4096], P(('dp', 'expert')), may hold values from -6 to 6
- routes: int32 [16384], P(('dp', 'expert')), may hold values from 0 to 31, as said below
- combine: float32 [16384], P(('dp', 'expert')), may hold values from 0.05 to 1
- expert_weights: bfloat16 [32, 3, 1536, 4096], P('expert', None, 'dp'), may hold values from -0.09375 to 0.09375
Outputs:
- combined: bfloat16 [16384, 4096], P(('dp', 'expert'))
- token_grad: bfloat16 [16384, 4096], P(('dp', 'expert'))
- combine_grad: float32 [16384], P(('dp', 'expert'))
Inputs may be any that keep to these rules, and one draw needn't show every extreme that they name: `routes`: among the 128 rows of every device, two experts, the same two on every device, are each named by exactly 8 rows, and every other expert by 3 or 4 rows.
All inputs are finite; a program needn't handle non-finite values.
Results may differ from a plain program's by a relative error of at most 0.015.
Values may be sent and summed in bfloat16 or wider, within the bound.
No kernel may reach another device: no remote copies, remote signals or barrier semaphores. Data moves between devices by JAX's collectives and lax.ppermute only.
A program may use at most 192 MiB of HBM per device.

v0:
```python
import jax
import jax.numpy as jnp
from jax import lax
from jax.sharding import PartitionSpec as P


def placement(member, slot_count):
    within = jnp.sum((jnp.cumsum(member, 0) - 1) * member, 1)
    owner_group = jnp.sum(member * lax.iota(jnp.int32, member.shape[1])[None, :], 1)
    is_used = jnp.sum(member, 1) > 0
    target = owner_group * slot_count + within
    buffer_cells = lax.iota(jnp.int32, member.shape[1] * slot_count)
    return ((buffer_cells[:, None] == target[None, :]) & is_used[None, :]).astype(jnp.bfloat16)


def spread(layout, row_block):
    return jnp.dot(layout, row_block, preferred_element_type=jnp.float32).astype(jnp.bfloat16)


def collect(layout, buffer_rows):
    return lax.dot_general(
        layout, buffer_rows, (((0,), (0,)), ((), ())), preferred_element_type=jnp.float32
    )


def group_rows(values):
    return lax.all_gather(values, "dp", axis=0, tiled=True)


def group_sum(values):
    return lax.psum_scatter(values.astype(jnp.bfloat16), "dp", scatter_dimension=0, tiled=True)


def exchange(rows, experts, model_width):
    return lax.all_to_all(
        rows.reshape(experts, -1, model_width), "expert", split_axis=0, concat_axis=0, tiled=True
    ).reshape(-1, model_width)


def forward_rows(row_block, matrices):
    gate_up = jnp.einsum("rd,kfd->krf", row_block, matrices[:2], preferred_element_type=jnp.float32)
    gate_act = gate_up[0]
    up_act = gate_up[1]
    hidden = (gate_act * jax.nn.sigmoid(gate_act) * up_act).astype(jnp.bfloat16)
    partial_out = jnp.dot(hidden, matrices[2], preferred_element_type=jnp.float32)
    return (gate_act, up_act, partial_out)


def backward_rows(row_block, gate_act, up_act, matrices):
    hidden_grad = lax.dot_general(
        row_block, matrices[2], (((1,), (1,)), ((), ())), preferred_element_type=jnp.float32
    )
    squashed = jax.nn.sigmoid(gate_act)
    gate_grad = (hidden_grad * up_act * squashed * (1.0 + gate_act * (1.0 - squashed))).astype(
        jnp.bfloat16
    )
    up_grad = (hidden_grad * gate_act * squashed).astype(jnp.bfloat16)
    both_grads = jnp.stack([gate_grad, up_grad])
    return jnp.einsum("krf,kfd->rd", both_grads, matrices[:2], preferred_element_type=jnp.float32)


def shards(tokens, cotangent, routes, combine, expert_weights):
    weights = expert_weights[0]
    tok_dev = tokens.shape[0]
    model_width = tokens.shape[1]
    experts = lax.axis_size("expert")
    capacity = 2 * tok_dev // experts
    chunks = 2
    chunk_slots = capacity // chunks
    labels = lax.iota(jnp.int32, experts)
    member = (routes[:, None] == labels[None, :]).astype(jnp.int32)
    layout = placement(member, capacity).reshape(experts, capacity, tok_dev)
    cotangent_wide = cotangent.astype(jnp.float32)
    out_grad = (combine[:, None] * cotangent_wide).astype(jnp.bfloat16)
    layouts = [
        layout[:, c * chunk_slots : (c + 1) * chunk_slots].reshape(-1, tok_dev)
        for c in range(chunks)
    ]
    tok_in = [group_rows(exchange(spread(lay, tokens), experts, model_width)) for lay in layouts]
    cot_in = [group_rows(exchange(spread(lay, out_grad), experts, model_width)) for lay in layouts]
    expert_out = None
    input_grad = None
    for c in range(chunks):
        gate_act, up_act, part = forward_rows(tok_in[c], weights)
        out_back = exchange(group_sum(part), experts, model_width)
        piece = collect(layouts[c], out_back)
        expert_out = piece if expert_out is None else expert_out + piece
        grad_part = backward_rows(cot_in[c], gate_act, up_act, weights)
        grad_back = exchange(group_sum(grad_part), experts, model_width)
        piece = collect(layouts[c], grad_back)
        input_grad = piece if input_grad is None else input_grad + piece
    combined = (combine[:, None] * expert_out).astype(jnp.bfloat16)
    combine_grad = jnp.sum(expert_out * cotangent_wide, 1)
    token_grad = input_grad.astype(jnp.bfloat16)
    return (combined, token_grad, combine_grad)


def solution(mesh):
    return jax.shard_map(
        shards,
        mesh=mesh,
        in_specs=(
            P(("dp", "expert"), None),
            P(("dp", "expert"), None),
            P(("dp", "expert")),
            P(("dp", "expert")),
            P("expert", None, "dp", None),
        ),
        out_specs=(P(("dp", "expert"), None), P(("dp", "expert"), None), P(("dp", "expert"))),
        check_vma=False,
    )
```

profile of v0, /device:TPU:1, one launch (start us, length us, event | category | flops | bytes accessed | tf_op | source)
XLA Modules:
  0.0 472.8 jit_solution(6738018536119864457)
XLA Ops:
  12.2 26.4 %all_to_all.40 = bf16[32,4,4096]{2,1,0:T(4,128)(2,1)} all-to-all(bf16[32,4,4096]{2,1,0:T(4,128)(2,1)S(1)} %reshape.93), channel_id=1, replica_groups=mesh['dp'=4,'expert'=32] {'expert'}, dimensions={0} | all-to-all | bytes 2097152 | tf_op jit(solution)/shard_map/all_to_all | solution.py:35
  38.7 2.1 reshape.94
  42.6 20.9 %all_to_all.41 = bf16[32,4,4096]{2,1,0:T(4,128)(2,1)S(1)} all-to-all(bf16[32,4,4096]{2,1,0:T(4,128)(2,1)} %reshape.99), channel_id=1, replica_groups=mesh['dp'=4,'expert'=32] {'expert'}, dimensions={0} | all-to-all | bytes 2097152 | tf_op jit(solution)/shard_map/all_to_all | solution.py:35
  65.6 20.7 %all_to_all.42 = bf16[32,4,4096]{2,1,0:T(4,128)(2,1)S(1)} all-to-all(bf16[32,4,4096]{2,1,0:T(4,128)(2,1)S(1)} %reshape.89), channel_id=1, replica_groups=mesh['dp'=4,'expert'=32] {'expert'}, dimensions={0} | all-to-all | bytes 2097152 | tf_op jit(solution)/shard_map/all_to_all | solution.py:35
  88.3 20.7 %all_to_all.43 = bf16[32,4,4096]{2,1,0:T(4,128)(2,1)S(1)} all-to-all(bf16[32,4,4096]{2,1,0:T(4,128)(2,1)S(1)} %reshape.96), channel_id=1, replica_groups=mesh['dp'=4,'expert'=32] {'expert'}, dimensions={0} | all-to-all | bytes 2097152 | tf_op jit(solution)/shard_map/all_to_all | solution.py:35
  110.2 8.8 %fusion.32 = f32[2,512,384]{2,1,0:T(8,128)} fusion(bf16[1,3,384,4096]{3,2,1,0:T(8,128)(2,1)} %param.9, bf16[512,4096]{1,0:T(8,128)(2,1)} %all-gather.7.cloned.1.call-done), kind=kOutput, calls=%fused_computation.43 | convolution fusion | flops 3221225472 | bytes 12058624 | tf_op jit(solution)/shard_map/rd,kfd->krf/dot_general | solution.py:41
  119.0 18.0 %all-gather.11.cloned.1.call-done = bf16[512,4096]{1,0:T(8,128)(2,1)} async-done(((bf16[128,4096]{1,0:T(8,128)(2,1)}), bf16[512,4096]{1,0:T(8,128)(2,1)}) %all-gather.11.cloned.1.call-update) | async-done | bytes 4194320 | tf_op jit(solution)/shard_map/all_gather | solution.py:27
  137.0 6.0 %fusion.72 = (bf16[1,512,384]{2,1,0:T(8,128)(2,1)S(1)}, bf16[1,512,384]{2,1,0:T(8,128)(2,1)S(1)}) fusion(f32[2,512,384]{2,1,0:T(8,128)} %fusion.32, bf16[512,4096]{1,0:T(8,128)(2,1)} %all-gather.11.cloned.1.call-done, bf16[1,3,384,4096]{3,2,1,0:T(8,128)(2,1)} %param.9), kind=kOutput, calls=%fused_computation.87 | convolution fusion | flops 1613168640 | bytes 9699328 | tf_op jit(solution)/shard_map/dot_general | solution.py:50
  143.0 7.7 %bitcast_convert_fusion = bf16[512,4096]{1,0:T(8,128)(2,1)} fusion(bf16[1,3,384,4096]{3,2,1,0:T(8,128)(2,1)} %param.9, bf16[1,512,384]{2,1,0:T(8,128)(2,1)S(1)} %get-tuple-element.9, bf16[1,512,384]{2,1,0:T(8,128)(2,1)S(1)} %get-tuple-element.8), kind=kOutput, calls=%fused_computation | convolution fusion | flops 3223715840 | bytes 11272192 | tf_op jit(solution)/shard_map/krf,kfd->rd/dot_general | solution.py:59
  151.0 36.9 %all-gather.5.cloned.1.call-done = bf16[512,4096]{1,0:T(8,128)(2,1)} async-done(((bf16[128,4096]{1,0:T(8,128)(2,1)}), bf16[512,4096]{1,0:T(8,128)(2,1)}) %all-gather.5.cloned.1.call-update) | async-done | bytes 4194320 | tf_op jit(solution)/shard_map/all_gather | solution.py:27
  187.9 8.7 %fusion.27 = f32[2,512,384]{2,1,0:T(8,128)} fusion(bf16[1,3,384,4096]{3,2,1,0:T(8,128)(2,1)} %param.9, bf16[512,4096]{1,0:T(8,128)(2,1)} %all-gather.5.cloned.1.call-done), kind=kOutput, calls=%fused_computation.42 | convolution fusion | flops 3221225472 | bytes 12058624 | tf_op jit(solution)/shard_map/rd,kfd->krf/dot_general | solution.py:41
  196.6 41.5 %all-gather.9.cloned.1.call-done = bf16[512,4096]{1,0:T(8,128)(2,1)} async-done(((bf16[128,4096]{1,0:T(8,128)(2,1)}), bf16[512,4096]{1,0:T(8,128)(2,1)}) %all-gather.9.cloned.1.call-update) | async-done | bytes 4194320 | tf_op jit(solution)/shard_map/all_gather | solution.py:27
  238.0 6.0 %fusion.71 = (bf16[1,512,384]{2,1,0:T(8,128)(2,1)S(1)}, bf16[1,512,384]{2,1,0:T(8,128)(2,1)S(1)}) fusion(f32[2,512,384]{2,1,0:T(8,128)} %fusion.27, bf16[512,4096]{1,0:T(8,128)(2,1)} %all-gather.9.cloned.1.call-done, bf16[1,3,384,4096]{3,2,1,0:T(8,128)(2,1)} %param.9), kind=kOutput, calls=%fused_computation.86 | convolution fusion | flops 1613168640 | bytes 9699328 | tf_op jit(solution)/shard_map/dot_general | solution.py:50
  244.0 7.7 %bitcast_convert_fusion.1 = bf16[512,4096]{1,0:T(8,128)(2,1)} fusion(bf16[1,3,384,4096]{3,2,1,0:T(8,128)(2,1)} %param.9, bf16[1,512,384]{2,1,0:T(8,128)(2,1)S(1)} %get-tuple-element.7, bf16[1,512,384]{2,1,0:T(8,128)(2,1)S(1)} %get-tuple-element.6), kind=kOutput, calls=%fused_computation.1 | convolution fusion | flops 3223715840 | bytes 11272192 | tf_op jit(solution)/shard_map/krf,kfd->rd/dot_general | solution.py:59
  251.8 6.7 %convolution_convert_fusion = bf16[512,4096]{1,0:T(8,128)(2,1)} fusion(bf16[1,3,384,4096]{3,2,1,0:T(8,128)(2,1)} %param.9, f32[2,512,384]{2,1,0:T(8,128)} %fusion.32), kind=kOutput, calls=%fused_computation.8 | convolution fusion | flops 1613889536 | bytes 8912896 | tf_op jit(solution)/shard_map/dot_general | solution.py:45
  258.6 6.8 %convolution_convert_fusion.1 = bf16[512,4096]{1,0:T(8,128)(2,1)} fusion(bf16[1,3,384,4096]{3,2,1,0:T(8,128)(2,1)} %param.9, f32[2,512,384]{2,1,0:T(8,128)} %fusion.27), kind=kOutput, calls=%fused_computation.9 | convolution fusion | flops 1613889536 | bytes 8912896 | tf_op jit(solution)/shard_map/dot_general | solution.py:45
  265.5 22.0 %reduce-scatter.11.cloned.1.call-done = bf16[128,4096]{1,0:T(8,128)(2,1)} async-done(((bf16[512,4096]{1,0:T(8,128)(2,1)}), bf16[128,4096]{1,0:T(8,128)(2,1)}) %reduce-scatter.11.cloned.1.call-update) | async-done | bytes 1048592 | tf_op jit(solution)/shard_map/reduce_scatter | solution.py:31
  287.5 2.2 reshape.101
  289.7 7.6 %all-to-all-start.7 = ((bf16[32,4,4096]{2,1,0:T(4,128)(2,1)}), bf16[32,4,4096]{2,1,0:T(4,128)(2,1)S(1)}, u32[]{:S(2)}, u32[]{:S(2)}) async-start(bf16[32,4,4096]{2,1,0:T(4,128)(2,1)} %reshape.101), calls=%async_computation.11 | async-start | bytes 2097152 | tf_op jit(solution)/shard_map/all_to_all | solution.py:35
  297.4 39.1 %reduce-scatter.9.cloned.1.call-done = bf16[128,4096]{1,0:T(8,128)(2,1)} async-done(((bf16[512,4096]{1,0:T(8,128)(2,1)}), bf16[128,4096]{1,0:T(8,128)(2,1)}) %reduce-scatter.9.cloned.1.call-update) | async-done | bytes 1048592 | tf_op jit(solution)/shard_map/reduce_scatter | solution.py:31
  336.5 2.2 reshape.98
  338.7 7.7 %all-to-all-start.5 = ((bf16[32,4,4096]{2,1,0:T(4,128)(2,1)}), bf16[32,4,4096]{2,1,0:T(4,128)(2,1)S(1)}, u32[]{:S(2)}, u32[]{:S(2)}) async-start(bf16[32,4,4096]{2,1,0:T(4,128)(2,1)} %reshape.98), calls=%async_computation.8 | async-start | bytes 2097152 | tf_op jit(solution)/shard_map/all_to_all | solution.py:35
  346.4 39.0 %reduce-scatter.7.cloned.1.call-done = bf16[128,4096]{1,0:T(8,128)(2,1)} async-done(((bf16[512,4096]{1,0:T(8,128)(2,1)}), bf16[128,4096]{1,0:T(8,128)(2,1)}) %reduce-scatter.7.cloned.1.call-update) | async-done | bytes 1048592 | tf_op jit(solution)/shard_map/reduce_scatter | solution.py:31
  385.4 2.2 reshape.95
  388.7 7.7 %all-to-all-start.3 = ((bf16[32,4,4096]{2,1,0:T(4,128)(2,1)}), bf16[32,4,4096]{2,1,0:T(4,128)(2,1)S(1)}, u32[]{:S(2)}, u32[]{:S(2)}) async-start(bf16[32,4,4096]{2,1,0:T(4,128)(2,1)} %reshape.95), calls=%async_computation.5 | async-start | bytes 2097152 | tf_op jit(solution)/shard_map/all_to_all | solution.py:35
  396.3 38.2 %reduce-scatter.5.cloned.1.call-done = bf16[128,4096]{1,0:T(8,128)(2,1)} async-done(((bf16[512,4096]{1,0:T(8,128)(2,1)}), bf16[128,4096]{1,0:T(8,128)(2,1)}) %reduce-scatter.5.cloned.1.call-update) | async-done | bytes 1048592 | tf_op jit(solution)/shard_map/reduce_scatter | solution.py:31
  434.5 2.2 reshape.91
  436.8 7.7 %all-to-all-start.1 = ((bf16[32,4,4096]{2,1,0:T(4,128)(2,1)}), bf16[32,4,4096]{2,1,0:T(4,128)(2,1)}, u32[]{:S(2)}, u32[]{:S(2)}) async-start(bf16[32,4,4096]{2,1,0:T(4,128)(2,1)} %reshape.91), calls=%async_computation.2 | async-start | bytes 2097152 | tf_op jit(solution)/shard_map/all_to_all | solution.py:35
  445.4 2.2 convolution_bitcast_fusion.2
  447.6 1.9 fusion.8
  449.5 11.9 %all-to-all-done.1 = bf16[32,4,4096]{2,1,0:T(4,128)(2,1)} async-done(((bf16[32,4,4096]{2,1,0:T(4,128)(2,1)}), bf16[32,4,4096]{2,1,0:T(4,128)(2,1)}, u32[]{:S(2)}, u32[]{:S(2)}) %all-to-all-start.1) | async-done | bytes 1048608 | tf_op jit(solution)/shard_map/all_to_all | solution.py:35
  461.4 4.6 fusion.22
  (54 shorter events, 14.4 us)
Async XLA Ops:
  7.2 2.1 copy-start
  7.2 103.0 %all-gather.7.cloned.1.call-start = ((), (), s32[]{:S(2)}) async-start(), calls=%async_computation.14 | async-start | bytes 5242880 | tf_op jit(solution)/shard_map/all_gather | solution.py:27
  10.7 30.2 %copy-start.2 = (bf16[128,4096]{1,0:T(8,128)(2,1)S(1)}, bf16[128,4096]{1,0:T(8,128)(2,1)}, u32[]{:S(2)}) copy-start(bf16[128,4096]{1,0:T(8,128)(2,1)} %param.6) | copy-start | bytes 3145732
  10.7 30.2 %copy-start.5 = (f32[128]{0:T(128)S(1)}, f32[128]{0:T(128)}, u32[]{:S(2)}) copy-start(f32[128]{0:T(128)} %param.8) | copy-start | bytes 1540
  40.8 96.2 %all-gather.11.cloned.1.call-start = ((), (), s32[]{:S(2)}) async-start(), calls=%async_computation.18 | async-start | bytes 5242880 | tf_op jit(solution)/shard_map/all_gather | solution.py:27
  64.6 123.3 %all-gather.5.cloned.1.call-start = ((), (), s32[]{:S(2)}) async-start(), calls=%async_computation.12 | async-start | bytes 5242880 | tf_op jit(solution)/shard_map/all_gather | solution.py:27
  87.3 150.7 %all-gather.9.cloned.1.call-start = ((), (), s32[]{:S(2)}) async-start(), calls=%async_computation.16 | async-start | bytes 5242880 | tf_op jit(solution)/shard_map/all_gather | solution.py:27
  110.1 177.4 %reduce-scatter.11.cloned.1.call-start = ((), (), s32[]{:S(2)}) async-start(), calls=%async_computation.19 | async-start | bytes 5242880 | tf_op jit(solution)/shard_map/reduce_scatter | solution.py:31
  150.8 185.7 %reduce-scatter.9.cloned.1.call-start = ((), (), s32[]{:S(2)}) async-start(), calls=%async_computation.17 | async-start | bytes 5242880 | tf_op jit(solution)/shard_map/reduce_scatter | solution.py:31
  251.8 133.6 %reduce-scatter.7.cloned.1.call-start = ((), (), s32[]{:S(2)}) async-start(), calls=%async_computation.15 | async-start | bytes 5242880 | tf_op jit(solution)/shard_map/reduce_scatter | solution.py:31
  258.6 175.9 %reduce-scatter.5.cloned.1.call-start = ((), (), s32[]{:S(2)}) async-start(), calls=%async_computation.13 | async-start | bytes 5242880 | tf_op jit(solution)/shard_map/reduce_scatter | solution.py:31
  289.7 49.0 %all-to-all-start.7 = ((bf16[32,4,4096]{2,1,0:T(4,128)(2,1)}), bf16[32,4,4096]{2,1,0:T(4,128)(2,1)S(1)}, u32[]{:S(2)}, u32[]{:S(2)}) async-start(bf16[32,4,4096]{2,1,0:T(4,128)(2,1)} %reshape.101), calls=%async_computation.11 | async-start | bytes 2097152 | tf_op jit(solution)/shard_map/all_to_all | solution.py:35
  338.7 48.9 %all-to-all-start.5 = ((bf16[32,4,4096]{2,1,0:T(4,128)(2,1)}), bf16[32,4,4096]{2,1,0:T(4,128)(2,1)S(1)}, u32[]{:S(2)}, u32[]{:S(2)}) async-start(bf16[32,4,4096]{2,1,0:T(4,128)(2,1)} %reshape.98), calls=%async_computation.8 | async-start | bytes 2097152 | tf_op jit(solution)/shard_map/all_to_all | solution.py:35
  387.6 1.0 copy-start.3
  388.7 48.1 %all-to-all-start.3 = ((bf16[32,4,4096]{2,1,0:T(4,128)(2,1)}), bf16[32,4,4096]{2,1,0:T(4,128)(2,1)S(1)}, u32[]{:S(2)}, u32[]{:S(2)}) async-start(bf16[32,4,4096]{2,1,0:T(4,128)(2,1)} %reshape.95), calls=%async_computation.5 | async-start | bytes 2097152 | tf_op jit(solution)/shard_map/all_to_all | solution.py:35
  436.8 24.7 %all-to-all-start.1 = ((bf16[32,4,4096]{2,1,0:T(4,128)(2,1)}), bf16[32,4,4096]{2,1,0:T(4,128)(2,1)}, u32[]{:S(2)}, u32[]{:S(2)}) async-start(bf16[32,4,4096]{2,1,0:T(4,128)(2,1)} %reshape.91), calls=%async_computation.2 | async-start | bytes 2097152 | tf_op jit(solution)/shard_map/all_to_all | solution.py:35
  444.5 3.2 copy-start.4
  445.4 20.6 %copy-start.1 = (bf16[128,4096]{1,0:T(8,128)(2,1)S(1)}, bf16[128,4096]{1,0:T(8,128)(2,1)}, u32[]{:S(2)}) copy-start(bf16[128,4096]{1,0:T(8,128)(2,1)} %param.5) | copy-start | bytes 3145732
Sparse Core Ops, SparseCore 0:
  40.9 45.7 all-gather.6
  88.4 48.5 all-gather.10
  139.3 48.5 all-gather.4
  189.4 48.5 all-gather.8
  240.3 47.1 reduce-scatter.10
  289.9 46.5 reduce-scatter.8
  338.9 46.4 reduce-scatter.6
  387.9 46.5 reduce-scatter.4
where the time goes:
time: 474 us; the launch traced here: 473 us
  waiting for transfers between devices  247 us (52%)
  blocking collectives  88.6 us (19%)
  matrix products  70.8 us (15%)
  starting transfers between devices  31.2 us (7%)
  local copies, waits for them, and re-layouts  19.1 us (4%)
  between operations  14.4 us (3%)
    reduce_scatter x4, waiting for transfers between devices, group_sum(): lax.psum_scatter(values.astype(jnp.bfloat16), 'dp', scatter_dimension=0,...  138 us
    all_gather x4, waiting for transfers between devices, group_rows(): return lax.all_gather(values, 'dp', axis=0, tiled=True)  96.4 us
    all_to_all x4, blocking collectives, exchange(): lax.all_to_all(rows.reshape(experts, -1, model_width), 'expert', split_ax...  88.6 us
    all_to_all x4, starting transfers between devices, exchange(): lax.all_to_all(rows.reshape(experts, -1, model_width), 'expert', split_ax...  30.7 us
    dot_general x2, matrix products, forward_rows(): jnp.einsum('rd,kfd->krf', row_block, matrices[:2], preferred_element_type...  17.4 us
    dot_general x2, matrix products, backward_rows(): jnp.einsum('krf,kfd->rd', both_grads, matrices[:2], preferred_element_typ...  15.5 us
    dot_general x2, matrix products, forward_rows(): jnp.dot(hidden, matrices[2], preferred_element_type=jnp.float32)  13.5 us
    reshape x8, local copies, waits for them, and re-layouts, exchange(): rows.reshape(experts, -1, model_width)  12.6 us
  transfers between devices with their start and end apart: 12, of which 8 were waited for; matrix products, arithmetic and copies ran while one was open for 17% of the time, Pallas kernels for 0%

commit v1 on v0

--- a/solution.py
+++ b/solution.py
@@ -24,7 +24,9 @@
 
 
 def group_rows(values):
-    return lax.all_gather(values, "dp", axis=0, tiled=True)
+    return jnp.concatenate(
+        lax.all_to_all(jnp.stack([values] * lax.axis_size("dp")), "dp", 0, 0), axis=0
+    )
 
 
 def group_sum(values):

time: 474 us -> 508 us (1.072)
  blocking collectives: 88.6 us -> 338 us
  waiting for transfers between devices: 247 us -> 54.9 us
  matrix products: 70.8 us -> 56.7 us
  starting transfers between devices: 31.2 us -> 20.3 us
    all_to_all x0 -> x4, blocking collectives: none -> 241 us  [group_rows(): lax.all_to_all(jnp.stack([values] * lax.axis_size('dp')), 'dp', 0, 0)]
    reduce_scatter x4, waiting for transfers between devices: 138 us -> 0.08 us  [group_sum(): lax.psum_scatter(values.astype(jnp.bfloat16), 'dp', scatter_dimension=0,...]
    all_gather x4 -> x0, waiting for transfers between devices: 96.4 us -> none  [group_rows(): return lax.all_gather(values, 'dp', axis=0, tiled=True)]
    all_to_all x4, waiting for transfers between devices: 11.9 us -> 54.8 us  [exchange(): lax.all_to_all(rows.reshape(experts, -1, model_width), 'expert', split_ax...]
    all_to_all x4, starting transfers between devices: 30.7 us -> 20.2 us  [exchange(): lax.all_to_all(rows.reshape(experts, -1, model_width), 'expert', split_ax...]
    all_to_all x4, blocking collectives: 88.6 us -> 96.6 us  [exchange(): lax.all_to_all(rows.reshape(experts, -1, model_width), 'expert', split_ax...]
    reshape x4 -> x0, local copies, waits for them, and re-layouts: 5.45 us -> none  [exchange(): return lax.all_to_all(rows.reshape(experts, -1, model_width), 'expert', s...]
    dot_general x2, matrix products: 15.5 us -> 10.2 us  [backward_rows(): jnp.einsum('krf,kfd->rd', both_grads, matrices[:2], preferred_element_typ...]
  transfers between devices with their start and end apart: 12 -> 8, of which waited for: 8 -> 4; matrix products, arithmetic and copies ran while one was open for 17% -> 11% of each run, Pallas kernels for 0% -> 0%
where the time goes in v1:
time: 508 us; the launch traced here: 507 us
  blocking collectives  338 us (67%)
  matrix products  56.7 us (11%)
  waiting for transfers between devices  54.9 us (11%)
  local copies, waits for them, and re-layouts  20.5 us (4%)
  starting transfers between devices  20.3 us (4%)
  between operations  14.2 us (3%)
    all_to_all x4, blocking collectives, group_rows(): lax.all_to_all(jnp.stack([values] * lax.axis_size('dp')), 'dp', 0, 0)  241 us
    all_to_all x4, blocking collectives, exchange(): lax.all_to_all(rows.reshape(experts, -1, model_width), 'expert', split_ax...  96.6 us
    all_to_all x4, waiting for transfers between devices, exchange(): lax.all_to_all(rows.reshape(experts, -1, model_width), 'expert', split_ax...  54.8 us
    all_to_all x4, starting transfers between devices, exchange(): lax.all_to_all(rows.reshape(experts, -1, model_width), 'expert', split_ax...  20.2 us
    dot_general x2, matrix products, forward_rows(): jnp.einsum('rd,kfd->krf', row_block, matrices[:2], preferred_element_type...  13.5 us
    dot_general x2, matrix products, forward_rows(): jnp.dot(hidden, matrices[2], preferred_element_type=jnp.float32)  12.5 us
    reshape x8, local copies, waits for them, and re-layouts, exchange(): rows.reshape(experts, -1, model_width)  10.7 us
    dot_general x2, matrix products, backward_rows(): jnp.einsum('krf,kfd->rd', both_grads, matrices[:2], preferred_element_typ...  10.2 us
  transfers between devices with their start and end apart: 8, of which 4 were waited for; matrix products, arithmetic and copies ran while one was open for 11% of the time, Pallas kernels for 0%

profile of v1, /device:TPU:1, one launch (start us, length us, event | category | flops | bytes accessed | tf_op | source)
XLA Modules:
  0.0 506.6 jit_solution(8110158204753588301)
XLA Ops:
  10.2 26.3 %all_to_all.60 = bf16[32,4,4096]{2,1,0:T(4,128)(2,1)S(1)} all-to-all(bf16[32,4,4096]{2,1,0:T(4,128)(2,1)S(1)} %reshape.97), channel_id=1, replica_groups=mesh['dp'=4,'expert'=32] {'expert'}, dimensions={0} | all-to-all | bytes 2097152 | tf_op jit(solution)/shard_map/all_to_all | solution.py:37
  37.2 52.3 %all_to_all.61 = bf16[4,128,4096]{2,1,0:T(8,128)(2,1)S(1)} all-to-all(bf16[4,128,4096]{2,1,0:T(8,128)(2,1)S(1)} %stack.30), channel_id=1, replica_groups=mesh['dp'=4,'expert'=32] {'dp'}, dimensions={0} | all-to-all | bytes 8388608 | tf_op jit(solution)/shard_map/all_to_all | solution.py:28
  89.5 6.7 %fusion.25 = f32[2,512,384]{2,1,0:T(8,128)S(1)} fusion(bf16[512,4096,1]{1,0,2:T(8,128)(2,1)S(1)} %bitcast.156, bf16[1,3,384,4096]{3,2,1,0:T(8,128)(2,1)} %param.9), kind=kOutput, calls=%fused_computation.40 | convolution fusion | flops 3221225472 | bytes 12058624 | tf_op jit(solution)/shard_map/rd,kfd->krf/dot_general | solution.py:43
  97.5 6.2 %convolution_convert_fusion.1 = bf16[512,4096]{1,0:T(8,128)(2,1)} fusion(bf16[1,3,384,4096]{3,2,1,0:T(8,128)(2,1)} %param.9, f32[2,512,384]{2,1,0:T(8,128)S(1)} %fusion.25), kind=kOutput, calls=%fused_computation.9 | convolution fusion | flops 1613889536 | bytes 8912896 | tf_op jit(solution)/shard_map/dot_general | solution.py:47
  104.7 21.5 %all_to_all.62 = bf16[32,4,4096]{2,1,0:T(4,128)(2,1)S(1)} all-to-all(bf16[32,4,4096]{2,1,0:T(4,128)(2,1)S(1)} %reshape.101), channel_id=1, replica_groups=mesh['dp'=4,'expert'=32] {'expert'}, dimensions={0} | all-to-all | bytes 2097152 | tf_op jit(solution)/shard_map/all_to_all | solution.py:37
  126.9 64.2 %all_to_all.63 = bf16[4,128,4096]{2,1,0:T(8,128)(2,1)S(1)} all-to-all(bf16[4,128,4096]{2,1,0:T(8,128)(2,1)S(1)} %stack.31), channel_id=1, replica_groups=mesh['dp'=4,'expert'=32] {'dp'}, dimensions={0} | all-to-all | bytes 8388608 | tf_op jit(solution)/shard_map/all_to_all | solution.py:28
  191.2 6.7 %fusion.28 = f32[2,512,384]{2,1,0:T(8,128)S(1)} fusion(bf16[512,4096,1]{1,0,2:T(8,128)(2,1)S(1)} %bitcast.157, bf16[1,3,384,4096]{3,2,1,0:T(8,128)(2,1)} %param.9), kind=kOutput, calls=%fused_computation.41 | convolution fusion | flops 3221225472 | bytes 12058624 | tf_op jit(solution)/shard_map/rd,kfd->krf/dot_general | solution.py:43
  199.1 6.2 %convolution_convert_fusion = bf16[512,4096]{1,0:T(8,128)(2,1)} fusion(bf16[1,3,384,4096]{3,2,1,0:T(8,128)(2,1)} %param.9, f32[2,512,384]{2,1,0:T(8,128)S(1)} %fusion.28), kind=kOutput, calls=%fused_computation.8 | convolution fusion | flops 1613889536 | bytes 8912896 | tf_op jit(solution)/shard_map/dot_general | solution.py:47
  207.5 24.4 %all_to_all.64 = bf16[32,4,4096]{2,1,0:T(4,128)(2,1)} all-to-all(bf16[32,4,4096]{2,1,0:T(4,128)(2,1)S(1)} %reshape.107), channel_id=1, replica_groups=mesh['dp'=4,'expert'=32] {'expert'}, dimensions={0} | all-to-all | bytes 2097152 | tf_op jit(solution)/shard_map/all_to_all | solution.py:37
  231.9 1.4 stack_reshape.11
  233.8 61.8 %all_to_all.65 = bf16[4,128,4096]{2,1,0:T(8,128)(2,1)S(1)} all-to-all(bf16[4,128,4096]{2,1,0:T(8,128)(2,1)S(1)} %stack.36), channel_id=1, replica_groups=mesh['dp'=4,'expert'=32] {'dp'}, dimensions={0} | all-to-all | bytes 8388608 | tf_op jit(solution)/shard_map/all_to_all | solution.py:28
  295.6 4.6 fusion.66
  300.2 5.1 %bitcast_convert_fusion = bf16[512,4096]{1,0:T(8,128)(2,1)} fusion(bf16[1,3,384,4096]{3,2,1,0:T(8,128)(2,1)S(1)} %bitcast.163, bf16[1,512,384]{2,1,0:T(8,128)(2,1)S(1)} %get-tuple-element.9, bf16[1,512,384]{2,1,0:T(8,128)(2,1)S(1)} %get-tuple-element.8), kind=kOutput, calls=%fused_computation | convolution fusion | flops 3223715840 | bytes 11272192 | tf_op jit(solution)/shard_map/krf,kfd->rd/dot_general | solution.py:61
  306.4 24.4 %all_to_all.66 = bf16[32,4,4096]{2,1,0:T(4,128)(2,1)} all-to-all(bf16[32,4,4096]{2,1,0:T(4,128)(2,1)S(1)} %reshape.104), channel_id=1, replica_groups=mesh['dp'=4,'expert'=32] {'expert'}, dimensions={0} | all-to-all | bytes 2097152 | tf_op jit(solution)/shard_map/all_to_all | solution.py:37
  332.7 63.0 %all_to_all.67 = bf16[4,128,4096]{2,1,0:T(8,128)(2,1)S(1)} all-to-all(bf16[4,128,4096]{2,1,0:T(8,128)(2,1)S(1)} %stack.32), channel_id=1, replica_groups=mesh['dp'=4,'expert'=32] {'dp'}, dimensions={0} | all-to-all | bytes 8388608 | tf_op jit(solution)/shard_map/all_to_all | solution.py:28
  395.6 4.6 fusion.65
  400.2 5.1 %bitcast_convert_fusion.1 = bf16[512,4096]{1,0:T(8,128)(2,1)} fusion(bf16[1,3,384,4096]{3,2,1,0:T(8,128)(2,1)S(1)} %bitcast.165, bf16[1,512,384]{2,1,0:T(8,128)(2,1)S(1)} %get-tuple-element.7, bf16[1,512,384]{2,1,0:T(8,128)(2,1)S(1)} %get-tuple-element.6), kind=kOutput, calls=%fused_computation.1 | convolution fusion | flops 3223715840 | bytes 11272192 | tf_op jit(solution)/shard_map/krf,kfd->rd/dot_general | solution.py:61
  405.4 2.2 reshape.99
  407.6 7.6 %all-to-all-start.2 = ((bf16[32,4,4096]{2,1,0:T(4,128)(2,1)}), bf16[32,4,4096]{2,1,0:T(4,128)(2,1)S(1)}, u32[]{:S(2)}, u32[]{:S(2)}) async-start(bf16[32,4,4096]{2,1,0:T(4,128)(2,1)} %reshape.99), calls=%async_computation.3 | async-start | bytes 2097152 | tf_op jit(solution)/shard_map/all_to_all | solution.py:37
  415.2 2.2 reshape.103
  417.4 14.6 %all-to-all-done.2 = bf16[32,4,4096]{2,1,0:T(4,128)(2,1)S(1)} async-done(((bf16[32,4,4096]{2,1,0:T(4,128)(2,1)}), bf16[32,4,4096]{2,1,0:T(4,128)(2,1)S(1)}, u32[]{:S(2)}, u32[]{:S(2)}) %all-to-all-start.2) | async-done | bytes 1048608 | tf_op jit(solution)/shard_map/all_to_all | solution.py:37
  433.1 4.0 all-to-all-start.5
  437.1 2.3 reshape.109
  439.3 14.6 %all-to-all-done.5 = bf16[32,4,4096]{2,1,0:T(4,128)(2,1)S(1)} async-done(((bf16[32,4,4096]{2,1,0:T(4,128)(2,1)}), bf16[32,4,4096]{2,1,0:T(4,128)(2,1)S(1)}, u32[]{:S(2)}, u32[]{:S(2)}) %all-to-all-start.5) | async-done | bytes 1048608 | tf_op jit(solution)/shard_map/all_to_all | solution.py:37
  453.9 4.0 all-to-all-start.11
  457.9 2.2 reshape.106
  460.2 14.6 %all-to-all-done.11 = bf16[32,4,4096]{2,1,0:T(4,128)(2,1)S(1)} async-done(((bf16[32,4,4096]{2,1,0:T(4,128)(2,1)}), bf16[32,4,4096]{2,1,0:T(4,128)(2,1)S(1)}, u32[]{:S(2)}, u32[]{:S(2)}) %all-to-all-start.11) | async-done | bytes 1048608 | tf_op jit(solution)/shard_map/all_to_all | solution.py:37
  474.8 4.7 all-to-all-start.8
  480.4 2.2 convolution_bitcast_fusion
  482.7 2.7 fusion.20
  485.4 10.9 %all-to-all-done.8 = bf16[32,4,4096]{2,1,0:T(4,128)(2,1)} async-done(((bf16[32,4,4096]{2,1,0:T(4,128)(2,1)}), bf16[32,4,4096]{2,1,0:T(4,128)(2,1)}, u32[]{:S(2)}, u32[]{:S(2)}) %all-to-all-start.8) | async-done | bytes 1048608 | tf_op jit(solution)/shard_map/all_to_all | solution.py:37
  496.3 3.8 fusion.8
  (72 shorter events, 15.2 us)
Async XLA Ops:
  7.2 2.1 copy-start
  7.2 398.2 %reduce-scatter.5.cloned.1.call-start = ((), (), s32[]{:S(2)}) async-start(), calls=%async_computation.16 | async-start | bytes 5242880 | tf_op jit(solution)/shard_map/reduce_scatter | solution.py:33
  96.3 1.2 copy-start.6
  103.7 311.5 %reduce-scatter.7.cloned.1.call-start = ((), (), s32[]{:S(2)}) async-start(), calls=%async_computation.17 | async-start | bytes 5242880 | tf_op jit(solution)/shard_map/reduce_scatter | solution.py:33
  197.9 1.2 copy-start.8
  205.4 1.2 copy-start.2
  205.4 1.2 copy-start.5
  205.4 231.6 %reduce-scatter.11.cloned.1.call-start = ((), (), s32[]{:S(2)}) async-start(), calls=%async_computation.19 | async-start | bytes 5242880 | tf_op jit(solution)/shard_map/reduce_scatter | solution.py:33
  233.8 61.8 %copy-start.9 = (f32[2,512,384]{2,1,0:T(8,128)S(1)}, f32[2,512,384]{2,1,0:T(8,128)}, u32[]{:S(2)}) copy-start(f32[2,512,384]{2,1,0:T(8,128)} %copy-done.8) | copy-start | bytes 4718596
  233.8 66.4 %slice-start = ((s8[9437184]{0:T(1024)(128)(4,1)}), s8[1048576]{0:T(1024)(128)(4,1)S(1)}, s32[]{:S(2)}) async-start(s8[9437184]{0:T(1024)(128)(4,1)} %bitcast.162), calls=%async_computation.20 | async-start | bytes 2097152
  233.8 66.4 %slice-start.1 = ((s8[9437184]{0:T(1024)(128)(4,1)}), s8[4194304]{0:T(1024)(128)(4,1)S(1)}, s32[]{:S(2)}) async-start(s8[9437184]{0:T(1024)(128)(4,1)} %bitcast.162), calls=%async_computation.21 | async-start | bytes 8388608
  295.6 4.6 slice-start.2
  305.4 152.5 %reduce-scatter.9.cloned.1.call-start = ((), (), s32[]{:S(2)}) async-start(), calls=%async_computation.18 | async-start | bytes 5242880 | tf_op jit(solution)/shard_map/reduce_scatter | solution.py:33
  332.6 63.0 %copy-start.7 = (f32[2,512,384]{2,1,0:T(8,128)S(1)}, f32[2,512,384]{2,1,0:T(8,128)}, u32[]{:S(2)}) copy-start(f32[2,512,384]{2,1,0:T(8,128)} %copy-done.6) | copy-start | bytes 4718596
  332.6 67.6 %slice-start.3 = ((s8[9437184]{0:T(1024)(128)(4,1)}), s8[1048576]{0:T(1024)(128)(4,1)S(1)}, s32[]{:S(2)}) async-start(s8[9437184]{0:T(1024)(128)(4,1)} %bitcast.164), calls=%async_computation.23 | async-start | bytes 2097152
  332.6 67.6 %slice-start.4 = ((s8[9437184]{0:T(1024)(128)(4,1)}), s8[4194304]{0:T(1024)(128)(4,1)S(1)}, s32[]{:S(2)}) async-start(s8[9437184]{0:T(1024)(128)(4,1)} %bitcast.164), calls=%async_computation.24 | async-start | bytes 8388608
  395.6 4.6 slice-start.5
  407.6 24.5 %all-to-all-start.2 = ((bf16[32,4,4096]{2,1,0:T(4,128)(2,1)}), bf16[32,4,4096]{2,1,0:T(4,128)(2,1)S(1)}, u32[]{:S(2)}, u32[]{:S(2)}) async-start(bf16[32,4,4096]{2,1,0:T(4,128)(2,1)} %reshape.99), calls=%async_computation.3 | async-start | bytes 2097152 | tf_op jit(solution)/shard_map/all_to_all | solution.py:37
  432.1 1.0 copy-start.3
  433.1 20.9 %all-to-all-start.5 = ((bf16[32,4,4096]{2,1,0:T(4,128)(2,1)}), bf16[32,4,4096]{2,1,0:T(4,128)(2,1)S(1)}, u32[]{:S(2)}, u32[]{:S(2)}) async-start(bf16[32,4,4096]{2,1,0:T(4,128)(2,1)} %reshape.103), calls=%async_computation.7 | async-start | bytes 2097152 | tf_op jit(solution)/shard_map/all_to_all | solution.py:37
  453.9 20.9 %all-to-all-start.11 = ((bf16[32,4,4096]{2,1,0:T(4,128)(2,1)}), bf16[32,4,4096]{2,1,0:T(4,128)(2,1)S(1)}, u32[]{:S(2)}, u32[]{:S(2)}) async-start(bf16[32,4,4096]{2,1,0:T(4,128)(2,1)} %reshape.109), calls=%async_computation.15 | async-start | bytes 2097152 | tf_op jit(solution)/shard_map/all_to_all | solution.py:37
  474.8 21.4 %all-to-all-start.8 = ((bf16[32,4,4096]{2,1,0:T(4,128)(2,1)}), bf16[32,4,4096]{2,1,0:T(4,128)(2,1)}, u32[]{:S(2)}, u32[]{:S(2)}) async-start(bf16[32,4,4096]{2,1,0:T(4,128)(2,1)} %reshape.106), calls=%async_computation.11 | async-start | bytes 2097152 | tf_op jit(solution)/shard_map/all_to_all | solution.py:37
  479.5 3.2 copy-start.4
  480.4 19.7 %copy-start.1 = (bf16[128,4096]{1,0:T(8,128)(2,1)S(1)}, bf16[128,4096]{1,0:T(8,128)(2,1)}, u32[]{:S(2)}) copy-start(bf16[128,4096]{1,0:T(8,128)(2,1)} %param.5) | copy-start | bytes 3145732
Sparse Core Ops, SparseCore 0:
  103.8 66.5 reduce-scatter.4
  205.5 63.6 reduce-scatter.6
  305.5 65.5 reduce-scatter.10
  405.4 46.1 reduce-scatter.8
